TPU v7x, 256 devices: a whole 4x4x8 slice. The times are simulated.
256 devices in a mesh: tile: 64 (over x, z, core), row: 4 (over y).
Axes of the slice: x: 4, y: 4, z: 8, core: 2. Of those that a mesh axis runs over, the one named last changes fastest.
Arguments:
- amplitudes: float32 [576, 64, 256], P('tile'), may hold values from -6 to 6
- integrals: float32 [4, 4096, 128, 256], P('row', 'tile'), may hold values from -0.0390625 to 0.0390625
- slot_ab: int32 [4, 4096], P('row', 'tile'), may hold values from 0 to 17
- slot_cd: int32 [4, 4096], P('row', 'tile'), may hold values from 0 to 575, as said below
- live_count: int32 [4, 64], P('row', 'tile'), may hold values from 1 to 64, as said below
- pair_list: int32 [64, 2], replicated, may hold values from 0 to 127, as said below
Outputs:
- symmetrized: float32 [64, 96, 96], P('tile', 'row')
Inputs may be any that keep to these rules, and one draw needn't show every extreme that they name: `slot_cd`: slot s of row index r belongs to tile index k = s // 64; its cd tile is held in amplitudes by tile index k - 1, k or k + 1, taken cyclically over the tile axis (cd tile c is held by tile index c // 9). `live_count`: slots at or after a device's count are unused. In every row index some device uses all 64 slots. `pair_list`: the rows are distinct pairs (i, j) with i != j, and for every row the reversed pair (j, i) is also a row.
All inputs are finite; a program needn't handle non-finite values.
Results may differ from a plain program's by a relative error of at most 0.0003.
Values sent between devices are 32-bit elements; how exact they have to be, the bound alone decides.
No kernel may reach another device: no remote copies, remote signals or barrier semaphores. Data moves between devices by JAX's collectives and lax.ppermute only.
A program may use at most 64 MiB of HBM per device.

v0:
```python
import jax
import jax.numpy as jnp
from jax import lax
from jax.sharding import PartitionSpec as P

TS = 16
ATS = 8
SLAB = 96


def padded(x, sides, width):
    for axis, dim in sides:
        size, length = (lax.axis_size(axis), x.shape[dim])
        up = [(i, (i + 1) % size) for i in range(size)]
        down = [(j, i) for i, j in up]
        last = lax.slice_in_dim(x, length - width, length, axis=dim)
        first = lax.slice_in_dim(x, 0, width, axis=dim)
        before = lax.ppermute(last, axis, up)
        after = lax.ppermute(first, axis, down)
        x = jnp.concatenate([before, x, after], axis=dim)
    return x


def find_mirror(pair_list):
    first_orb = pair_list[:, 0]
    second = pair_list[:, 1]
    matches = (first_orb[:, None] == second[None, :]) & (second[:, None] == first_orb[None, :])
    columns = jnp.arange(pair_list.shape[0], dtype=jnp.int32)
    return jnp.sum(jnp.where(matches, columns[None, :], 0), axis=1)


def to_grid(totals, a_tiles, b_tiles):
    pair_count = totals.shape[1]
    shaped = totals.reshape(a_tiles, b_tiles, pair_count, ATS, TS)
    return jnp.transpose(shaped, (2, 0, 3, 1, 4)).reshape(pair_count, a_tiles * ATS, b_tiles * TS)


def shards(amplitudes, integrals, slot_ab, slot_cd, live_count, pair_list):
    highest = lax.Precision.HIGHEST
    tile_size = lax.axis_size("tile")
    row_size = lax.axis_size("row")
    tile_index = lax.axis_index("tile")
    shard_tiles = amplitudes.shape[0]
    pair_count = amplitudes.shape[1]
    extended = padded(amplitudes, (("tile", 0),), shard_tiles)
    blocks_all = integrals[0]
    ab_local = slot_ab[0]
    cd_global = slot_cd[0]
    owner_tile = cd_global // shard_tiles
    offset = (owner_tile - tile_index + 1 + tile_size) % tile_size
    ext_index = offset * shard_tiles + cd_global % shard_tiles
    live_total = live_count[0, 0]
    a_tiles = SLAB // (row_size * ATS)
    b_tiles = SLAB // TS
    tiles_ab = a_tiles * b_tiles
    block_width = integrals.shape[2]
    group_size = 8

    def block_step(block_index, totals):
        first_slot = block_index * group_size
        picked = lax.dynamic_slice_in_dim(ext_index, first_slot, group_size)
        ab_tiles = lax.dynamic_slice_in_dim(ab_local, first_slot, group_size)
        blocks = lax.dynamic_slice_in_dim(blocks_all, first_slot, group_size, 0)
        live_mask = (first_slot + jnp.arange(group_size, dtype=jnp.int32) < live_total).astype(
            jnp.float32
        )
        amp_tiles = jnp.take(extended, picked, axis=0)
        products = jnp.einsum(
            "spw,sbw->spb", amp_tiles, blocks, precision=highest, preferred_element_type=jnp.float32
        )
        one_hot = (ab_tiles[:, None] == jnp.arange(tiles_ab, dtype=jnp.int32)[None, :]).astype(
            jnp.float32
        ) * live_mask[:, None]
        return totals + jnp.einsum(
            "se,spb->epb", one_hot, products, precision=highest, preferred_element_type=jnp.float32
        )

    turn_count = (live_total + group_size - 1) // group_size
    start_totals = jnp.zeros((tiles_ab, pair_count, block_width), jnp.float32)
    totals = lax.fori_loop(0, turn_count, block_step, start_totals)
    whole_term = to_grid(totals, a_tiles, b_tiles)
    mirror = find_mirror(pair_list)
    reduced = lax.psum_scatter(whole_term, "tile", scatter_dimension=0, tiled=True)
    exchanged = lax.all_to_all(reduced, "row", split_axis=2, concat_axis=1, tiled=True)
    turned = jnp.transpose(exchanged, (0, 2, 1))
    everyone = lax.all_gather(turned, "tile", axis=0, tiled=True)
    local_pairs = reduced.shape[0]
    wanted = lax.dynamic_slice_in_dim(mirror, tile_index * local_pairs, local_pairs)
    return reduced + jnp.take(everyone, wanted, axis=0)


def solution(mesh):
    return jax.shard_map(
        shards,
        mesh=mesh,
        in_specs=(
            P("tile", None, None),
            P("row", "tile", None, None),
            P("row", "tile"),
            P("row", "tile"),
            P("row", "tile"),
            P(),
        ),
        out_specs=P("tile", "row", None),
        check_vma=False,
    )
```

profile of v0, /device:TPU:1, one launch (start us, length us, event | category | flops | bytes accessed | tf_op | source)
XLA Modules:
  0.0 267.6 jit_solution(6142205821760800485)
XLA Ops:
  6.5 3.0 %collective-permute-start = (f32[9,64,256]{2,1,0:T(8,128)}, f32[9,64,256]{2,1,0:T(8,128)S(1)}, u32[]{:S(2)}, u32[]{:S(2)}) collective-permute-start(f32[9,64,256]{2,1,0:T(8,128)} %param.8), channel_id=1, source_target_pairs={{0,4},{4,8},{8,12},{12,16},{16,20},{20,24},{24,28},{28,32},{32,36}... | collective-permute-start | bytes 1769480 | tf_op jit(solution)/shard_map/ppermute | solution.py:18
  10.4 0.7 fusion.16
  11.1 5.6 %collective-permute-done = f32[9,64,256]{2,1,0:T(8,128)S(1)} collective-permute-done((f32[9,64,256]{2,1,0:T(8,128)}, f32[9,64,256]{2,1,0:T(8,128)S(1)}, u32[]{:S(2)}, u32[]{:S(2)}) %collective-permute-start) | collective-permute-done | bytes 589856 | tf_op jit(solution)/shard_map/ppermute | solution.py:18
  16.7 2.7 collective-permute-done.1
  19.4 1.2 pad_maximum_fusion
  20.7 39.7 %while.11 = (s32[]{:T(128)}, f32[18,64,128]{2,0,1:T(8,128)S(1)}, s32[]{:T(128)}, s32[64]{0:T(128)S(1)}, s32[]{:T(128)}, /*index=5*/s32[64]{0:T(128)S(1)}, f32[27...) while((s32[]{:T(128)}, f32[18,64,128]{2,0,1:T(8,128)S(1)}, ...), condition=%wide.region_1.2_spmd, body=%wide.region_0.1_spmd.sunk | while | flops 215762288 | bytes 4329959 | solution.py:80
  20.7 0.7 compare_and_fusion.2
  21.4 0.6 gather_fusion
  22.0 2.5 fusion.28
  24.6 1.0 convolution_add_fusion.2
  25.6 0.7 compare_and_fusion.2
  26.4 0.6 gather_fusion
  27.0 2.5 fusion.28
  29.6 1.0 convolution_add_fusion.2
  30.6 0.7 compare_and_fusion.2
  31.3 0.6 gather_fusion
  31.9 2.5 fusion.28
  34.5 1.0 convolution_add_fusion.2
  35.6 0.7 compare_and_fusion.2
  36.3 0.6 gather_fusion
  36.9 2.5 fusion.28
  39.5 1.0 convolution_add_fusion.2
  40.5 0.7 compare_and_fusion.2
  41.3 0.6 gather_fusion
  41.9 2.5 fusion.28
  44.5 1.0 convolution_add_fusion.2
  45.5 0.7 compare_and_fusion.2
  46.2 0.6 gather_fusion
  46.8 2.5 fusion.28
  49.4 1.0 convolution_add_fusion.2
  50.5 0.7 compare_and_fusion.2
  51.2 0.6 gather_fusion
  51.8 2.5 fusion.28
  54.4 1.0 convolution_add_fusion.2
  55.4 0.7 compare_and_fusion.2
  56.8 2.5 fusion.28
  59.4 1.0 convolution_add_fusion.2
  60.9 1.2 copy.29
  62.2 128.7 %reduce-scatter.4.cloned.1.call-done = f32[1,24,96]{2,1,0:T(8,128)} async-done(((f32[64,24,96]{2,1,0:T(8,128)}), f32[1,24,96]{2,1,0:T(8,128)}) %reduce-scatter.4.cloned.1.call-update) | async-done | bytes 9232
  190.9 0.8 copy.30
  192.2 0.7 reduce
  192.9 0.7 reshape.79
  193.6 4.0 %all-to-all-start = ((f32[4,1,576]{2,1,0:T(1,128)}), f32[4,1,576]{2,1,0:T(1,128)S(1)}, u32[]{:S(2)}, u32[]{:S(2)}) async-start(f32[4,1,576]{2,1,0:T(1,128)} %reshape.79), calls=%async_computation | async-start | bytes 20480 | tf_op jit(solution)/shard_map/all_to_all | solution.py:84
  197.8 0.7 dynamic_slice.12
  200.3 1.4 all-to-all-done
  201.8 0.6 reduce.1
  202.8 56.7 %all_gather.3 = f32[64,24,96]{2,1,0:T(8,128)S(1)} all-gather(f32[1,24,96]{2,1,0:T(8,128)S(1)} %bitcast.48), channel_id=1, replica_groups=mesh['tile'=64,'row'=4] {'tile'}, dimensions={0}, use_global_device_ids=true | all-gather | bytes 599040 | tf_op jit(solution)/shard_map/all_gather | solution.py:86
  259.4 1.3 fusion.14
  (34 shorter events, 3.1 us)
Async XLA Ops:
  6.5 184.4 %reduce-scatter.4.cloned.1.call-start = ((), (), s32[]{:S(2)}) async-start(), calls=%async_computation.2 | async-start | bytes 798720
  6.5 10.2 %collective-permute-start = (f32[9,64,256]{2,1,0:T(8,128)}, f32[9,64,256]{2,1,0:T(8,128)S(1)}, u32[]{:S(2)}, u32[]{:S(2)}) collective-permute-start(f32[9,64,256]{2,1,0:T(8,128)} %param.8), channel_id=1, source_target_pairs={{0,4},{4,8},{8,12},{12,16},{16,20},{20,24},{24,28},{28,32},{32,36}... | collective-permute-start | bytes 1769480 | tf_op jit(solution)/shard_map/ppermute | solution.py:18
  9.6 9.8 %collective-permute-start.1 = (f32[9,64,256]{2,1,0:T(8,128)}, f32[9,64,256]{2,1,0:T(8,128)S(1)}, u32[]{:S(2)}, u32[]{:S(2)}) collective-permute-start(f32[9,64,256]{2,1,0:T(8,128)} %param.8), channel_id=1, source_target_pairs={{4,0},{8,4},{12,8},{16,12},{20,16},{24,20},{28,24},{32,28},{36,32}... | collective-permute-start | bytes 1769480 | tf_op jit(solution)/shard_map/ppermute | solution.py:19
  11.1 9.6 %copy-start.1 = (s32[1,64]{1,0:T(1,128)S(1)}, s32[1,64]{1,0:T(1,128)}, u32[]{:S(2)}) copy-start(s32[1,64]{1,0:T(1,128)} %param.10) | copy-start | bytes 772
  60.9 1.3 copy-start
  193.6 8.2 %all-to-all-start = ((f32[4,1,576]{2,1,0:T(1,128)}), f32[4,1,576]{2,1,0:T(1,128)S(1)}, u32[]{:S(2)}, u32[]{:S(2)}) async-start(f32[4,1,576]{2,1,0:T(1,128)} %reshape.79), calls=%async_computation | async-start | bytes 20480 | tf_op jit(solution)/shard_map/all_to_all | solution.py:84
Sparse Core Ops, SparseCore 0:
  62.3 128.5 reduce-scatter.3
where the time goes:
time: 268 us
  waiting for transfers between devices  138 us (51%)
  blocking collectives  56.7 us (21%)
  matrix products  28.3 us (11%)
  between operations  16.1 us (6%)
  other arithmetic  10.5 us (4%)
  local copies, waits for them, and re-layouts  10.1 us (4%)
  starting transfers between devices  7.18 us (3%)
    unnamed x2, waiting for transfers between devices  129 us
    all_gather x1, blocking collectives, shards(): everyone = lax.all_gather(turned, 'tile', axis=0, tiled=True)  56.7 us
    dot_general x8, matrix products, block_step(): jnp.einsum('spw,sbw->spb', amp_tiles, blocks, precision=highest, preferre...  20.3 us
    dot_general x8, matrix products, block_step(): jnp.einsum('se,spb->epb', one_hot, products, precision=highest, preferred...  8.01 us
    and x8, other arithmetic, block_step(): amp_tiles = jnp.take(extended, picked, axis=0)  5.82 us
    ppermute x1, waiting for transfers between devices, padded(): before = lax.ppermute(last, axis, up)  5.59 us
  transfers between devices with their start and end apart: 4, of which 4 were waited for; matrix products, arithmetic and copies ran while one was open for 1% of the time, Pallas kernels for 0%

commit v1 on v0

--- a/solution.py
+++ b/solution.py
@@ -83,7 +83,15 @@
     reduced = lax.psum_scatter(whole_term, "tile", scatter_dimension=0, tiled=True)
     exchanged = lax.all_to_all(reduced, "row", split_axis=2, concat_axis=1, tiled=True)
     turned = jnp.transpose(exchanged, (0, 2, 1))
-    everyone = lax.all_gather(turned, "tile", axis=0, tiled=True)
+    everyone = jnp.concatenate(
+        jax.lax.all_to_all(
+            jnp.stack([turned for _ in range(jax.lax.axis_size("tile"))]),
+            axis_name="tile",
+            split_axis=0,
+            concat_axis=0,
+        ),
+        axis=0,
+    )
     local_pairs = reduced.shape[0]
     wanted = lax.dynamic_slice_in_dim(mirror, tile_index * local_pairs, local_pairs)
     return reduced + jnp.take(everyone, wanted, axis=0)

time: 268 us -> 249 us (0.929)
  blocking collectives: 56.7 us -> 7.96 us
  waiting for transfers between devices: 138 us -> 157 us
  starting transfers between devices: 7.18 us -> 17.8 us
    all_gather x1 -> x0, blocking collectives: 56.7 us -> none  [shards(): everyone = lax.all_gather(turned, 'tile', axis=0, tiled=True)]
    all_to_all x1, waiting for transfers between devices: 1.44 us -> 20.2 us  [shards(): jax.lax.all_to_all(jnp.stack([turned for _ in range(jax.lax.axis_size('ti...]
    all_to_all x1, starting transfers between devices: 3.97 us -> 14.6 us  [shards(): jax.lax.all_to_all(jnp.stack([turned for _ in range(jax.lax.axis_size('ti...]
    all_to_all x0 -> x1, blocking collectives: none -> 7.96 us  [shards(): lax.all_to_all(reduced, 'row', split_axis=2, concat_axis=1, tiled=True)]
where the time goes in v1:
time: 249 us; the launch traced here: 248 us
  waiting for transfers between devices  157 us (63%)
  matrix products  28.3 us (11%)
  starting transfers between devices  17.8 us (7%)
  between operations  16.1 us (6%)
  local copies, waits for them, and re-layouts  10.5 us (4%)
  other arithmetic  9.99 us (4%)
  blocking collectives  7.96 us (3%)
    unnamed x2, waiting for transfers between devices  129 us
    dot_general x8, matrix products, block_step(): jnp.einsum('spw,sbw->spb', amp_tiles, blocks, precision=highest, preferre...  20.3 us
    all_to_all x1, waiting for transfers between devices, shards(): jax.lax.all_to_all(jnp.stack([turned for _ in range(jax.lax.axis_size('ti...  20.2 us
    all_to_all x1, starting transfers between devices, shards(): jax.lax.all_to_all(jnp.stack([turned for _ in range(jax.lax.axis_size('ti...  14.6 us
    dot_general x8, matrix products, block_step(): jnp.einsum('se,spb->epb', one_hot, products, precision=highest, preferred...  8.01 us
    all_to_all x1, blocking collectives, shards(): lax.all_to_all(reduced, 'row', split_axis=2, concat_axis=1, tiled=True)  7.96 us
    and x8, other arithmetic, block_step(): amp_tiles = jnp.take(extended, picked, axis=0)  5.82 us
    ppermute x1, waiting for transfers between devices, padded(): before = lax.ppermute(last, axis, up)  5.59 us
  transfers between devices with their start and end apart: 4, of which 4 were waited for; matrix products, arithmetic and copies ran while one was open for 1% of the time, Pallas kernels for 0%

profile of v1, /device:TPU:1, one launch (start us, length us, event | category | flops | bytes accessed | tf_op | source)
XLA Modules:
  0.0 248.1 jit_solution(10191683840620149851)
XLA Ops:
  6.5 3.0 %collective-permute-start = (f32[9,64,256]{2,1,0:T(8,128)}, f32[9,64,256]{2,1,0:T(8,128)S(1)}, u32[]{:S(2)}, u32[]{:S(2)}) collective-permute-start(f32[9,64,256]{2,1,0:T(8,128)} %param.8), channel_id=1, source_target_pairs={{0,4},{4,8},{8,12},{12,16},{16,20},{20,24},{24,28},{28,32},{32,36}... | collective-permute-start | bytes 1769480 | tf_op jit(solution)/shard_map/ppermute | solution.py:18
  10.4 0.7 fusion.15
  11.1 5.6 %collective-permute-done = f32[9,64,256]{2,1,0:T(8,128)S(1)} collective-permute-done((f32[9,64,256]{2,1,0:T(8,128)}, f32[9,64,256]{2,1,0:T(8,128)S(1)}, u32[]{:S(2)}, u32[]{:S(2)}) %collective-permute-start) | collective-permute-done | bytes 589856 | tf_op jit(solution)/shard_map/ppermute | solution.py:18
  16.7 2.7 %collective-permute-done.1 = f32[9,64,256]{2,1,0:T(8,128)S(1)} collective-permute-done((f32[9,64,256]{2,1,0:T(8,128)}, f32[9,64,256]{2,1,0:T(8,128)S(1)}, u32[]{:S(2)}, u32[]{:S(2)}) %collective-permute-start.1) | collective-permute-done | bytes 589856 | tf_op jit(solution)/shard_map/ppermute | solution.py:19
  19.4 1.2 pad_maximum_fusion
  20.7 39.7 %while.11 = (s32[]{:T(128)}, f32[18,64,128]{2,0,1:T(8,128)S(1)}, s32[]{:T(128)}, s32[64]{0:T(128)S(1)}, s32[]{:T(128)}, /*index=5*/s32[64]{0:T(128)S(1)}, f32[27...) while((s32[]{:T(128)}, f32[18,64,128]{2,0,1:T(8,128)S(1)}, ...), condition=%wide.region_1.2_spmd, body=%wide.region_0.1_spmd.sunk | while | flops 215762288 | bytes 4329959 | solution.py:80
  20.7 0.7 compare_and_fusion.2
  21.4 0.6 gather_fusion
  22.0 2.5 %fusion.27 = f32[8,64,128]{2,1,0:T(8,128)S(1)} fusion(f32[64,128,256]{2,1,0:T(8,128)} %get-tuple-element.168, s32[]{:T(128)S(6)} %select_n.87, f32[8,64,256]{2,1,0:T(8,128)S(1)} %gather_fusion, pred[8]{0:T(512)(128)(4,1)S(1)} %get-tuple-element.135), kind=kOutput, calls=%fused_computation.2.clone.1 | convolution fusion | flops 201457664 | bytes 1835020 | tf_op jit(solution)/shard_map/while/body/spw,sbw->spb/dot_general | solution.py:68
  24.6 1.0 convolution_add_fusion.2
  25.6 0.7 compare_and_fusion.2
  26.4 0.6 gather_fusion
  27.0 2.5 %fusion.27 = f32[8,64,128]{2,1,0:T(8,128)S(1)} fusion(f32[64,128,256]{2,1,0:T(8,128)} %get-tuple-element.168, s32[]{:T(128)S(6)} %select_n.87, f32[8,64,256]{2,1,0:T(8,128)S(1)} %gather_fusion, pred[8]{0:T(512)(128)(4,1)S(1)} %get-tuple-element.135), kind=kOutput, calls=%fused_computation.2.clone.1 | convolution fusion | flops 201457664 | bytes 1835020 | tf_op jit(solution)/shard_map/while/body/spw,sbw->spb/dot_general | solution.py:68
  29.6 1.0 convolution_add_fusion.2
  30.6 0.7 compare_and_fusion.2
  31.3 0.6 gather_fusion
  31.9 2.5 %fusion.27 = f32[8,64,128]{2,1,0:T(8,128)S(1)} fusion(f32[64,128,256]{2,1,0:T(8,128)} %get-tuple-element.168, s32[]{:T(128)S(6)} %select_n.87, f32[8,64,256]{2,1,0:T(8,128)S(1)} %gather_fusion, pred[8]{0:T(512)(128)(4,1)S(1)} %get-tuple-element.135), kind=kOutput, calls=%fused_computation.2.clone.1 | convolution fusion | flops 201457664 | bytes 1835020 | tf_op jit(solution)/shard_map/while/body/spw,sbw->spb/dot_general | solution.py:68
  34.5 1.0 convolution_add_fusion.2
  35.6 0.7 compare_and_fusion.2
  36.3 0.6 gather_fusion
  36.9 2.5 %fusion.27 = f32[8,64,128]{2,1,0:T(8,128)S(1)} fusion(f32[64,128,256]{2,1,0:T(8,128)} %get-tuple-element.168, s32[]{:T(128)S(6)} %select_n.87, f32[8,64,256]{2,1,0:T(8,128)S(1)} %gather_fusion, pred[8]{0:T(512)(128)(4,1)S(1)} %get-tuple-element.135), kind=kOutput, calls=%fused_computation.2.clone.1 | convolution fusion | flops 201457664 | bytes 1835020 | tf_op jit(solution)/shard_map/while/body/spw,sbw->spb/dot_general | solution.py:68
  39.5 1.0 convolution_add_fusion.2
  40.5 0.7 compare_and_fusion.2
  41.3 0.6 gather_fusion
  41.9 2.5 %fusion.27 = f32[8,64,128]{2,1,0:T(8,128)S(1)} fusion(f32[64,128,256]{2,1,0:T(8,128)} %get-tuple-element.168, s32[]{:T(128)S(6)} %select_n.87, f32[8,64,256]{2,1,0:T(8,128)S(1)} %gather_fusion, pred[8]{0:T(512)(128)(4,1)S(1)} %get-tuple-element.135), kind=kOutput, calls=%fused_computation.2.clone.1 | convolution fusion | flops 201457664 | bytes 1835020 | tf_op jit(solution)/shard_map/while/body/spw,sbw->spb/dot_general | solution.py:68
  44.5 1.0 convolution_add_fusion.2
  45.5 0.7 compare_and_fusion.2
  46.2 0.6 gather_fusion
  46.8 2.5 %fusion.27 = f32[8,64,128]{2,1,0:T(8,128)S(1)} fusion(f32[64,128,256]{2,1,0:T(8,128)} %get-tuple-element.168, s32[]{:T(128)S(6)} %select_n.87, f32[8,64,256]{2,1,0:T(8,128)S(1)} %gather_fusion, pred[8]{0:T(512)(128)(4,1)S(1)} %get-tuple-element.135), kind=kOutput, calls=%fused_computation.2.clone.1 | convolution fusion | flops 201457664 | bytes 1835020 | tf_op jit(solution)/shard_map/while/body/spw,sbw->spb/dot_general | solution.py:68
  49.4 1.0 convolution_add_fusion.2
  50.5 0.7 compare_and_fusion.2
  51.2 0.6 gather_fusion
  51.8 2.5 %fusion.27 = f32[8,64,128]{2,1,0:T(8,128)S(1)} fusion(f32[64,128,256]{2,1,0:T(8,128)} %get-tuple-element.168, s32[]{:T(128)S(6)} %select_n.87, f32[8,64,256]{2,1,0:T(8,128)S(1)} %gather_fusion, pred[8]{0:T(512)(128)(4,1)S(1)} %get-tuple-element.135), kind=kOutput, calls=%fused_computation.2.clone.1 | convolution fusion | flops 201457664 | bytes 1835020 | tf_op jit(solution)/shard_map/while/body/spw,sbw->spb/dot_general | solution.py:68
  54.4 1.0 convolution_add_fusion.2
  55.4 0.7 compare_and_fusion.2
  56.8 2.5 %fusion.27 = f32[8,64,128]{2,1,0:T(8,128)S(1)} fusion(f32[64,128,256]{2,1,0:T(8,128)} %get-tuple-element.168, s32[]{:T(128)S(6)} %select_n.87, f32[8,64,256]{2,1,0:T(8,128)S(1)} %gather_fusion, pred[8]{0:T(512)(128)(4,1)S(1)} %get-tuple-element.135), kind=kOutput, calls=%fused_computation.2.clone.1 | convolution fusion | flops 201457664 | bytes 1835020 | tf_op jit(solution)/shard_map/while/body/spw,sbw->spb/dot_general | solution.py:68
  59.4 1.0 convolution_add_fusion.2
  60.9 1.2 copy.34
  62.2 128.7 %reduce-scatter.4.cloned.1.call-done = f32[1,24,96]{2,1,0:T(8,128)} async-done(((f32[64,24,96]{2,1,0:T(8,128)}), f32[1,24,96]{2,1,0:T(8,128)}) %reduce-scatter.4.cloned.1.call-update) | async-done | bytes 9232
  190.9 0.9 copy.35
  192.3 0.8 reduce
  193.2 8.0 %all_to_all.23 = f32[4,1,576]{2,1,0:T(1,128)S(1)} all-to-all(f32[4,1,576]{2,1,0:T(1,128)S(1)} %reshape.90), channel_id=1, replica_groups=mesh['tile'=64,'row'=4] {'row'}, dimensions={0} | all-to-all | bytes 18432 | tf_op jit(solution)/shard_map/all_to_all | solution.py:84
  201.1 0.7 reduce.1
  202.2 0.9 stack.2
  203.2 14.6 %all-to-all-start.1 = ((f32[64,1,24,96]{3,2,1,0:T(8,128)}), f32[64,1,24,96]{3,2,1,0:T(8,128)S(1)}, u32[]{:S(2)}, u32[]{:S(2)}) async-start(f32[64,1,24,96]{3,2,1,0:T(8,128)} %stack.2), calls=%async_computation.1 | async-start | bytes 1572864 | tf_op jit(solution)/shard_map/all_to_all | solution.py:87
  218.0 0.6 dynamic_slice.12
  220.5 20.2 %all-to-all-done.1 = f32[64,1,24,96]{3,2,1,0:T(8,128)S(1)} async-done(((f32[64,1,24,96]{3,2,1,0:T(8,128)}), f32[64,1,24,96]{3,2,1,0:T(8,128)S(1)}, u32[]{:S(2)}, u32[]{:S(2)}) %all-to-all-start.1) | async-done | bytes 589856 | tf_op jit(solution)/shard_map/all_to_all | solution.py:87
  240.7 0.6 bitcast_add_fusion
  (37 shorter events, 3.2 us)
Async XLA Ops:
  6.5 184.4 %reduce-scatter.4.cloned.1.call-start = ((), (), s32[]{:S(2)}) async-start(), calls=%async_computation.3 | async-start | bytes 798720
  6.5 10.2 %collective-permute-start = (f32[9,64,256]{2,1,0:T(8,128)}, f32[9,64,256]{2,1,0:T(8,128)S(1)}, u32[]{:S(2)}, u32[]{:S(2)}) collective-permute-start(f32[9,64,256]{2,1,0:T(8,128)} %param.8), channel_id=1, source_target_pairs={{0,4},{4,8},{8,12},{12,16},{16,20},{20,24},{24,28},{28,32},{32,36}... | collective-permute-start | bytes 1769480 | tf_op jit(solution)/shard_map/ppermute | solution.py:18
  9.6 9.8 %collective-permute-start.1 = (f32[9,64,256]{2,1,0:T(8,128)}, f32[9,64,256]{2,1,0:T(8,128)S(1)}, u32[]{:S(2)}, u32[]{:S(2)}) collective-permute-start(f32[9,64,256]{2,1,0:T(8,128)} %param.8), channel_id=1, source_target_pairs={{4,0},{8,4},{12,8},{16,12},{20,16},{24,20},{28,24},{32,28},{36,32}... | collective-permute-start | bytes 1769480 | tf_op jit(solution)/shard_map/ppermute | solution.py:19
  11.1 9.6 %copy-start.2 = (s32[1,64]{1,0:T(1,128)S(1)}, s32[1,64]{1,0:T(1,128)}, u32[]{:S(2)}) copy-start(s32[1,64]{1,0:T(1,128)} %param.10) | copy-start | bytes 772
  62.2 155.6 %copy-start.1 = (s32[64,2]{0,1:T(2,128)S(1)}, s32[64,2]{0,1:T(2,128)}, u32[]{:S(2)}) copy-start(s32[64,2]{0,1:T(2,128)} %param.13) | copy-start | bytes 1540
  190.9 49.8 %copy-start = (f32[1,24,96]{2,1,0:T(8,128)S(1)}, f32[1,24,96]{2,1,0:T(8,128)}, u32[]{:S(2)}) copy-start(f32[1,24,96]{2,1,0:T(8,128)} %reduce-scatter.4.cloned.1.call-done) | copy-start | bytes 27652
  203.2 37.5 %all-to-all-start.1 = ((f32[64,1,24,96]{3,2,1,0:T(8,128)}), f32[64,1,24,96]{3,2,1,0:T(8,128)S(1)}, u32[]{:S(2)}, u32[]{:S(2)}) async-start(f32[64,1,24,96]{3,2,1,0:T(8,128)} %stack.2), calls=%async_computation.1 | async-start | bytes 1572864 | tf_op jit(solution)/shard_map/all_to_all | solution.py:87
Sparse Core Ops, SparseCore 0:
  62.3 128.5 reduce-scatter.3
